TPU v7x, 32 devices: a whole 2x2x4 slice. The times are simulated.
32 devices in a mesh: groups: 2 (over y), dp: 16 (over z, x, core).
Axes of the slice: x: 2, y: 2, z: 4, core: 2. Of those that a mesh axis runs over, the one named last changes fastest.
Arguments:
- queries: bfloat16 [8192, 2048], P(('groups', 'dp')), parts along dimension 0, may hold values from -6 to 6
- grad_out: bfloat16 [8192, 2048], P(('groups', 'dp')), parts along dimension 0, may hold values from -60 to 60
- params: float32 [4096, 2048], P(('groups', 'dp')), parts along dimension 0, may hold values from -0.0625 to 0.0625
- first_moment: float32 [4096, 2048], P(('groups', 'dp')), parts along dimension 0, may hold values from -6 to 6
- second_moment: float32 [4096, 2048], P(('groups', 'dp')), parts along dimension 0, may hold values from 0.05 to 0.08
- key_params: float32 [4096, 2048], P(('groups', 'dp')), parts along dimension 0, may hold values from -0.0625 to 0.0625
- keys: bfloat16 [4096, 2048], P(('groups', 'dp')), parts along dimension 0, may hold values from -6 to 6
- perm: int32 [4096], P('groups'), parts along dimension 0, may hold values from 0 to 2047, as said below
- inv_perm: int32 [4096], P('groups'), parts along dimension 0, may hold values from 0 to 2047, as said below
- bn_gain: float32 [4096], P('groups'), parts along dimension 0, may hold values from 0.25 to 1.75
- bn_shift: float32 [4096], P('groups'), parts along dimension 0, may hold values from -3 to 3
- queue: bfloat16 [16, 2048, 2048], P('groups', 'dp'), parts along dimension 0, may hold values from -6 to 6
- slot: int32 [1], replicated, may hold values from 0 to 7
Outputs:
- new_params: float32 [4096, 2048], P(('groups', 'dp')), parts along dimension 0
- new_first: float32 [4096, 2048], P(('groups', 'dp')), parts along dimension 0
- new_second: float32 [4096, 2048], P(('groups', 'dp')), parts along dimension 0
- new_key: float32 [4096, 2048], P(('groups', 'dp')), parts along dimension 0
- new_queue: bfloat16 [16, 2048, 2048], P('groups', 'dp'), parts along dimension 0
There are 2 independent parts, one for each index of `groups`. A program takes and returns all parts, laid end to end along the dimension named above; an argument that names none is the same for every part. Nothing has to cross between parts.
Inputs may be any that keep to these rules, and one draw needn't show every extreme that they name: perm is a permutation of 0 to 2047; each aligned block of 128 of its entries holds exactly 8 values from every aligned block of 128 values. inv_perm[perm[i]] = i for every i.
All inputs are finite; a program needn't handle non-finite values.
Results may differ from a plain program's by a relative error of at most 0.0025.
Values may be sent and summed in bfloat16 or wider, within the bound.
No kernel may reach another device: no remote copies, remote signals or barrier semaphores. Data moves between devices by JAX's collectives and lax.ppermute only.
A program may use at most 128 MiB of HBM per device.

v0:
```python
import jax
import jax.numpy as jnp
from jax import lax
from jax.sharding import PartitionSpec as P

norm_epsilon = 1e-05
adam_epsilon = 1e-08
bias_first = 1.0 - 0.9**10
bias_second = 1.0 - 0.999**10


def route(mapping, position, block_rows, per_peer):
    members = mapping.shape[0] // block_rows
    layout = mapping.reshape(members, block_rows)
    owned = (layout // block_rows == position).astype(jnp.int32)
    ordinal = jnp.cumsum(owned, axis=1) - 1
    destination = jnp.arange(members, dtype=jnp.int32)[:, None] * per_peer + ordinal
    destination = jnp.where(owned == 1, destination, members * per_peer)
    offsets = jnp.where(owned == 1, layout - position * block_rows, 0)
    send_index = (
        jnp.zeros((members * per_peer + 1,), jnp.int32)
        .at[destination.reshape(-1)]
        .set(offsets.reshape(-1))[: members * per_peer]
    )
    own_block = lax.dynamic_slice_in_dim(mapping, position * block_rows, block_rows)
    anchor = own_block // block_rows
    indicator = (anchor[:, None] == jnp.arange(members, dtype=jnp.int32)[None, :]).astype(jnp.int32)
    arrival = jnp.sum((jnp.cumsum(indicator, axis=0) - 1) * indicator, axis=1)
    return (send_index, anchor * per_peer + arrival)


def grad_term(queries, grad_out):
    return lax.dot_general(
        queries, grad_out, (((0,), (0,)), ((), ())), preferred_element_type=jnp.float32
    )


def adamw(gradient, params, first_moment, second_moment, key_params):
    new_first = 0.9 * first_moment + 0.1 * gradient
    new_second = 0.999 * second_moment + 0.001 * gradient * gradient
    update = new_first / bias_first / (jnp.sqrt(new_second / bias_second) + adam_epsilon)
    new_params = params - 0.05 * (update + 0.1 * params)
    new_key = 0.99 * key_params + 0.01 * new_params
    return (new_params, new_first, new_second, new_key)


def batch_norm(codes, bn_gain, bn_shift):
    values = codes.astype(jnp.float32)
    center = jnp.mean(values, axis=0)
    spread = jnp.mean(jnp.square(values - center), axis=0)
    return jax.nn.relu(
        (values - center) * lax.rsqrt(spread + norm_epsilon) * bn_gain + bn_shift
    ).astype(jnp.bfloat16)


def per_device(
    queries,
    grad_out,
    params,
    first_moment,
    second_moment,
    key_params,
    keys,
    perm,
    inv_perm,
    bn_gain,
    bn_shift,
    queue,
    slot,
):
    position = lax.axis_index("dp")
    members = lax.axis_size("dp")
    block_rows = keys.shape[0]
    per_peer = block_rows // members
    scaling = 1.0 / jnp.sqrt(jnp.float32(queries.shape[0] * members))
    send_forward, receive_forward = route(perm, position, block_rows, per_peer)
    send_back, receive_back = route(inv_perm, position, block_rows, per_peer)
    moved = lax.all_to_all(
        jnp.take(keys, send_forward, axis=0), "dp", split_axis=0, concat_axis=0, tiled=True
    )
    encoded_rows = jnp.take(moved, receive_forward, axis=0)
    gradient = (
        lax.psum_scatter(grad_term(queries, grad_out), "dp", scatter_dimension=0, tiled=True)
        * scaling
    )
    new_params, new_first, new_second, new_key = adamw(
        gradient, params, first_moment, second_moment, key_params
    )
    codes = jnp.dot(
        encoded_rows,
        lax.all_gather(new_key.astype(jnp.bfloat16), "dp", axis=0, tiled=True),
        preferred_element_type=jnp.float32,
    )
    codes = codes.astype(jnp.bfloat16)
    normed = batch_norm(codes, bn_gain, bn_shift)
    returned = lax.all_to_all(
        jnp.take(normed, send_back, axis=0), "dp", split_axis=0, concat_axis=0, tiled=True
    )
    restored = jnp.take(returned, receive_back, axis=0)
    new_queue = lax.dynamic_update_slice(
        queue, restored[None], (slot[0], jnp.int32(0), jnp.int32(0))
    )
    return (new_params, new_first, new_second, new_key, new_queue)


def solution(mesh):
    in_specs = (
        P(("groups", "dp"), None),
        P(("groups", "dp"), None),
        P(("groups", "dp"), None),
        P(("groups", "dp"), None),
        P(("groups", "dp"), None),
        P(("groups", "dp"), None),
        P(("groups", "dp"), None),
        P("groups"),
        P("groups"),
        P("groups"),
        P("groups"),
        P("groups", "dp", None),
        P(),
    )
    out_specs = (
        P(("groups", "dp"), None),
        P(("groups", "dp"), None),
        P(("groups", "dp"), None),
        P(("groups", "dp"), None),
        P("groups", "dp", None),
    )
    return jax.shard_map(
        per_device, mesh=mesh, in_specs=in_specs, out_specs=out_specs, check_vma=False
    )
```

profile of v0, /device:TPU:0, one launch (start us, length us, event | category | flops | bytes accessed | tf_op | source)
XLA Modules:
  0.0 325.0 jit_solution(14405362757740360536)
XLA Ops:
  7.2 0.0 copy-start
  7.2 0.0 copy-start.2
  7.2 0.0 reduce-scatter.2.cloned.1.call-start
  7.2 4.9 %copy.21 = bf16[8,128,2048]{2,1,0:T(8,128)(2,1)} copy(bf16[8,128,2048]{2,1,0:T(8,128)(2,1)} %param.26) | data formatting | bytes 8388608
  12.2 0.0 copy-done
  12.2 0.0 copy-done.2
  12.2 8.1 %fusion.29 = f32[2048,2048]{1,0:T(8,128)} fusion(bf16[256,2048]{1,0:T(8,128)(2,1)S(1)} %copy-done, bf16[256,2048]{1,0:T(8,128)(2,1)S(1)} %copy-done.2), kind=kOutput, calls=%fused_computation.102 | convolution fusion | flops 2147483648 | bytes 18874368 | tf_op jit(solution)/shard_map/dot_general | solution.py:33
  20.3 0.0 copy-start.3
  20.3 0.0 reduce-scatter.2.cloned.1.call-update
  20.3 0.0 copy-start.5
  20.3 0.0 copy-start.4
  20.3 0.0 copy-start.1
  20.3 0.0 all-gather.2.cloned.1.call-start
  20.4 181.3 %reduce-scatter.2.cloned.1.call-done = f32[128,2048]{1,0:T(8,128)} async-done(((f32[2048,2048]{1,0:T(8,128)}), f32[128,2048]{1,0:T(8,128)}) %reduce-scatter.2.cloned.1.call-update) | async-done | bytes 1048592 | tf_op jit(solution)/shard_map/reduce_scatter | solution.py:83
  201.7 0.0 copy-done.3
  201.7 5.1 %fusion.27 = (bf16[128,2048]{1,0:T(8,128)(2,1)}, f32[128,2048]{1,0:T(8,128)}, f32[128,2048]{1,0:T(8,128)}, f32[128,2048]{1,0:T(8,128)}, f32[128,2048]{1,0:T(8,128)}) fusion(f32[128,2048]{1,0:T(8,128)S(1)} %copy-done.3, f32[128,2048]{1,0:T(8,128)} %param.17, f32[128,2048]{1,0:T(8,128)} %reduce-scatter.2.cloned.1.call-done, f32[128,2048]{1,0:T(8,128)} %param.18, ...), kind=kLoop, calls=%fused_computation.100 | loop fusion | flops 5242880 | bytes 9961472 | tf_op jit(solution)/shard_map/convert_element_type | solution.py:91
  206.8 0.0 all-gather.2.cloned.1.call-update
  206.8 0.0 copy-done.5
  206.9 0.3 reduce_window_sum.34
  207.1 0.0 copy-done.4
  207.2 0.3 reduce_window_sum.36
  207.4 0.1 subtract_select_fusion
  207.5 8.0 %scatter_custom_fusion = s32[129]{0:T(256)S(1)} fusion(s32[2048]{0:T(1024)S(1)} %get-tuple-element.25, s32[2048]{0:T(1024)S(1)} %get-tuple-element.26, s32[]{:T(128)} %constant.105.clone.1), kind=kCustom, calls=%fused_computation.97 | custom fusion | bytes 520 | tf_op jit(solution)/shard_map/scatter | solution.py:23
  215.6 0.0 copy-done.1
  215.6 0.9 gather_fusion
  216.5 1.0 select_bitcast_fusion.1
  217.5 3.7 %all-to-all-start = ((bf16[16,8,2048]{2,1,0:T(8,128)(2,1)}), bf16[16,8,2048]{2,1,0:T(8,128)(2,1)S(1)}, u32[]{:S(2)}, u32[]{:S(2)}) async-start(bf16[16,8,2048]{2,1,0:T(8,128)(2,1)} %select_bitcast_fusion.1), calls=%async_computation.1 | async-start | bytes 1048576 | tf_op jit(solution)/shard_map/all_to_all | solution.py:78
  221.2 0.1 and_select_fusion
  221.3 0.1 fusion.5
  221.4 0.2 reduce_window_sum.35
  221.6 8.0 %scatter_custom_fusion.1 = s32[129]{0:T(256)S(1)} fusion(s32[2048]{0:T(1024)S(1)} %get-tuple-element.20, s32[2048]{0:T(1024)S(1)} %get-tuple-element.19, s32[]{:T(128)} %constant.105.clone.1), kind=kCustom, calls=%fused_computation.95 | custom fusion | bytes 520 | tf_op jit(solution)/shard_map/scatter | solution.py:23
  229.6 0.2 select_reduce_fusion.1
  229.8 14.4 %all-to-all-done = bf16[16,8,2048]{2,1,0:T(8,128)(2,1)S(1)} async-done(((bf16[16,8,2048]{2,1,0:T(8,128)(2,1)}), bf16[16,8,2048]{2,1,0:T(8,128)(2,1)S(1)}, u32[]{:S(2)}, u32[]{:S(2)}) %all-to-all-start) | async-done | bytes 524320 | tf_op jit(solution)/shard_map/all_to_all | solution.py:78
  244.2 0.9 gather_fusion.1
  245.2 46.1 %all-gather.2.cloned.1.call-done = bf16[2048,2048]{1,0:T(8,128)(2,1)} async-done(((bf16[128,2048]{1,0:T(8,128)(2,1)}), bf16[2048,2048]{1,0:T(8,128)(2,1)}) %all-gather.2.cloned.1.call-update) | async-done | bytes 8388624 | tf_op jit(solution)/shard_map/all_gather | solution.py:91
  291.3 0.0 copy-start.6
  291.3 0.0 copy-start.7
  291.3 4.7 %fusion.28 = (f32[2048]{0:T(1024)S(1)}, f32[128,2048]{1,0:T(8,128)S(1)}) fusion(bf16[2048,2048]{1,0:T(8,128)(2,1)} %all-gather.2.cloned.1.call-done, bf16[128,2048]{1,0:T(8,128)(2,1)S(1)} %gather_fusion.1, pred[128]{0:T(512)(128)(4,1)S(1)} %get-tuple-element.10), kind=kOutput, calls=%fused_computation.101 | convolution fusion | flops 1074788352 | bytes 9969792 | tf_op jit(solution)/shard_map/dot_general | solution.py:89
  296.0 0.1 multiply_reduce_fusion
  296.2 0.0 copy-done.6
  296.2 0.0 copy-done.7
  296.2 0.2 maximum_convert_fusion
  296.4 0.9 gather_fusion.2
  297.4 0.9 select_bitcast_fusion
  298.3 3.6 %all-to-all-start.1 = ((bf16[16,8,2048]{2,1,0:T(8,128)(2,1)}), bf16[16,8,2048]{2,1,0:T(8,128)(2,1)S(1)}, u32[]{:S(2)}, u32[]{:S(2)}) async-start(bf16[16,8,2048]{2,1,0:T(8,128)(2,1)} %select_bitcast_fusion), calls=%async_computation.2 | async-start | bytes 1048576 | tf_op jit(solution)/shard_map/all_to_all | solution.py:96
  301.8 0.1 fusion.4
  301.9 0.2 reduce_window_sum.37
  302.8 0.2 select_reduce_fusion
  303.0 13.3 %all-to-all-done.1 = bf16[16,8,2048]{2,1,0:T(8,128)(2,1)S(1)} async-done(((bf16[16,8,2048]{2,1,0:T(8,128)(2,1)}), bf16[16,8,2048]{2,1,0:T(8,128)(2,1)S(1)}, u32[]{:S(2)}, u32[]{:S(2)}) %all-to-all-start.1) | async-done | bytes 524320 | tf_op jit(solution)/shard_map/all_to_all | solution.py:96
  316.3 0.9 gather_fusion.3
  317.2 1.0 bitcast_dynamic-update-slice_fusion
  (13 shorter events, 0.1 us)
Async XLA Ops:
  7.2 5.0 %copy-start = (bf16[256,2048]{1,0:T(8,128)(2,1)S(1)}, bf16[256,2048]{1,0:T(8,128)(2,1)}, u32[]{:S(2)}) copy-start(bf16[256,2048]{1,0:T(8,128)(2,1)} %param.15) | copy-start | bytes 3145732
  7.2 5.0 %copy-start.2 = (bf16[256,2048]{1,0:T(8,128)(2,1)S(1)}, bf16[256,2048]{1,0:T(8,128)(2,1)}, u32[]{:S(2)}) copy-start(bf16[256,2048]{1,0:T(8,128)(2,1)} %param.16) | copy-start | bytes 3145732
  7.2 194.5 %reduce-scatter.2.cloned.1.call-start = ((), (), s32[]{:S(2)}) async-start(), calls=%async_computation.3 | async-start | bytes 17825792 | tf_op jit(solution)/shard_map/reduce_scatter | solution.py:83
  20.3 181.4 %copy-start.3 = (f32[128,2048]{1,0:T(8,128)S(1)}, f32[128,2048]{1,0:T(8,128)}, u32[]{:S(2)}) copy-start(f32[128,2048]{1,0:T(8,128)} %param.20) | copy-start | bytes 3145732
  20.3 186.5 %copy-start.5 = (s32[2048]{0:T(1024)S(1)}, s32[2048]{0:T(1024)}, u32[]{:S(2)}) copy-start(s32[2048]{0:T(1024)} %param.22) | copy-start | bytes 24580
  20.3 186.8 %copy-start.4 = (s32[2048]{0:T(1024)S(1)}, s32[2048]{0:T(1024)}, u32[]{:S(2)}) copy-start(s32[2048]{0:T(1024)} %param.23) | copy-start | bytes 24580
  20.3 195.3 %copy-start.1 = (bf16[128,2048]{1,0:T(8,128)(2,1)S(1)}, bf16[128,2048]{1,0:T(8,128)(2,1)}, u32[]{:S(2)}) copy-start(bf16[128,2048]{1,0:T(8,128)(2,1)} %param.21) | copy-start | bytes 1572868
  20.3 270.9 %all-gather.2.cloned.1.call-start = ((), (), s32[]{:S(2)}) async-start(), calls=%async_computation.4 | async-start | bytes 8912896 | tf_op jit(solution)/shard_map/all_gather | solution.py:91
  217.5 26.7 %all-to-all-start = ((bf16[16,8,2048]{2,1,0:T(8,128)(2,1)}), bf16[16,8,2048]{2,1,0:T(8,128)(2,1)S(1)}, u32[]{:S(2)}, u32[]{:S(2)}) async-start(bf16[16,8,2048]{2,1,0:T(8,128)(2,1)} %select_bitcast_fusion.1), calls=%async_computation.1 | async-start | bytes 1048576 | tf_op jit(solution)/shard_map/all_to_all | solution.py:78
  291.3 4.9 %copy-start.6 = (f32[2048]{0:T(1024)S(1)}, f32[2048]{0:T(1024)}, u32[]{:S(2)}) copy-start(f32[2048]{0:T(1024)} %param.25) | copy-start | bytes 24580
  291.3 4.9 %copy-start.7 = (f32[2048]{0:T(1024)S(1)}, f32[2048]{0:T(1024)}, u32[]{:S(2)}) copy-start(f32[2048]{0:T(1024)} %param.24) | copy-start | bytes 24580
  298.3 18.0 %all-to-all-start.1 = ((bf16[16,8,2048]{2,1,0:T(8,128)(2,1)}), bf16[16,8,2048]{2,1,0:T(8,128)(2,1)S(1)}, u32[]{:S(2)}, u32[]{:S(2)}) async-start(bf16[16,8,2048]{2,1,0:T(8,128)(2,1)} %select_bitcast_fusion), calls=%async_computation.2 | async-start | bytes 1048576 | tf_op jit(solution)/shard_map/all_to_all | solution.py:96
Sparse Core Ops, SparseCore 0:
  20.4 181.2 reduce-scatter.1
  206.9 84.2 all-gather.1
where the time goes:
time: 325 us
  waiting for transfers between devices  255 us (78%)
  local copies, waits for them, and re-layouts  24.8 us (8%)
  between operations  14.9 us (5%)
  matrix products  12.8 us (4%)
  other arithmetic  9.96 us (3%)
  starting transfers between devices  7.34 us (2%)
    reduce_scatter x1, waiting for transfers between devices, per_device(): lax.psum_scatter(grad_term(queries, grad_out), 'dp', scatter_dimension=0,...  181 us
    all_gather x1, waiting for transfers between devices, per_device(): lax.all_gather(new_key.astype(jnp.bfloat16), 'dp', axis=0, tiled=True)  46.1 us
    scatter x2, local copies, waits for them, and re-layouts, route(): send_index = jnp.zeros((members * per_peer + 1,), jnp.int32).at[destinati...  16.1 us
    all_to_all x1, waiting for transfers between devices, per_device(): lax.all_to_all(jnp.take(keys, send_forward, axis=0), 'dp', split_axis=0,...  14.4 us
    all_to_all x1, waiting for transfers between devices, per_device(): lax.all_to_all(jnp.take(normed, send_back, axis=0), 'dp', split_axis=0, c...  13.3 us
    dot_general x1, matrix products, grad_term(): lax.dot_general(queries, grad_out, (((0,), (0,)), ((), ())), preferred_el...  8.1 us
  transfers between devices with their start and end apart: 4, of which 4 were waited for; matrix products, arithmetic and copies ran while one was open for 6% of the time, Pallas kernels for 0%

commit v1 on v0

--- a/solution.py
+++ b/solution.py
@@ -7,6 +7,19 @@
 adam_epsilon = 1e-08
 bias_first = 1.0 - 0.9**10
 bias_second = 1.0 - 0.999**10
+
+
+def ring_gather(x, axis, dim):
+    ways = lax.axis_size(axis)
+    up = [(d, (d + 1) % ways) for d in range(ways)]
+    down = [(d, (d - 1) % ways) for d in range(ways)]
+    earlier, later = ([x], [x])
+    for _ in range(ways // 2):
+        earlier.append(lax.ppermute(earlier[-1], axis, up))
+    for _ in range((ways - 1) // 2):
+        later.append(lax.ppermute(later[-1], axis, down))
+    line = jnp.concatenate([*earlier[::-1], *later[1:]], axis=dim)
+    return jnp.roll(line, (lax.axis_index(axis) - ways // 2) * x.shape[dim], axis=dim)
 
 
 def route(mapping, position, block_rows, per_peer):
@@ -88,7 +101,7 @@
     )
     codes = jnp.dot(
         encoded_rows,
-        lax.all_gather(new_key.astype(jnp.bfloat16), "dp", axis=0, tiled=True),
+        ring_gather(new_key.astype(jnp.bfloat16), "dp", 0),
         preferred_element_type=jnp.float32,
     )
     codes = codes.astype(jnp.bfloat16)

time: 325 us -> 372 us (1.14)
  starting transfers between devices: 7.34 us -> 51.8 us
  local copies, waits for them, and re-layouts: 24.8 us -> 49 us
  waiting for transfers between devices: 255 us -> 234 us
    all_gather x1 -> x0, waiting for transfers between devices: 46.1 us -> none  [per_device(): lax.all_gather(new_key.astype(jnp.bfloat16), 'dp', axis=0, tiled=True)]
    ppermute x0 -> x15, waiting for transfers between devices: none -> 39.3 us  [the longest x8 39.3 us: ring_gather(): earlier.append(lax.ppermute(earlier[-1], axis, up))]
    ppermute x0 -> x15, starting transfers between devices: none -> 39.2 us  [the longest x7 28.5 us: ring_gather(): later.append(lax.ppermute(later[-1], axis, down))]
    unnamed x17 -> x56, local copies, waits for them, and re-layouts: 4.97 us -> 29.2 us
    all_to_all x1, waiting for transfers between devices: 14.4 us -> 0.01 us  [per_device(): lax.all_to_all(jnp.take(keys, send_forward, axis=0), 'dp', split_axis=0,...]
    all_to_all x1, starting transfers between devices: 3.69 us -> 9.02 us  [per_device(): lax.all_to_all(jnp.take(keys, send_forward, axis=0), 'dp', split_axis=0,...]
  transfers between devices with their start and end apart: 4 -> 18, of which waited for: 4 -> 7; matrix products, arithmetic and copies ran while one was open for 6% -> 9% of each run, Pallas kernels for 0% -> 0%
where the time goes in v1:
time: 372 us; the launch traced here: 371 us
  waiting for transfers between devices  234 us (63%)
  starting transfers between devices  51.8 us (14%)
  local copies, waits for them, and re-layouts  49 us (13%)
  between operations  15.3 us (4%)
  matrix products  10.8 us (3%)
  other arithmetic  9.7 us (3%)
    reduce_scatter x1, waiting for transfers between devices, per_device(): lax.psum_scatter(grad_term(queries, grad_out), 'dp', scatter_dimension=0,...  181 us
    ppermute x8, waiting for transfers between devices, ring_gather(): earlier.append(lax.ppermute(earlier[-1], axis, up))  39.3 us
    unnamed x56, local copies, waits for them, and re-layouts  29.2 us
    ppermute x7, starting transfers between devices, ring_gather(): later.append(lax.ppermute(later[-1], axis, down))  28.5 us
    scatter x2, local copies, waits for them, and re-layouts, route(): send_index = jnp.zeros((members * per_peer + 1,), jnp.int32).at[destinati...  16.1 us
    all_to_all x1, waiting for transfers between devices, per_device(): lax.all_to_all(jnp.take(normed, send_back, axis=0), 'dp', split_axis=0, c...  13.3 us
    ppermute x8, starting transfers between devices, ring_gather(): earlier.append(lax.ppermute(earlier[-1], axis, up))  10.7 us
    dot_general x1, matrix products, grad_term(): lax.dot_general(queries, grad_out, (((0,), (0,)), ((), ())), preferred_el...  9.44 us
  transfers between devices with their start and end apart: 18, of which 7 were waited for; matrix products, arithmetic and copies ran while one was open for 9% of the time, Pallas kernels for 0%

profile of v1, /device:TPU:0, one launch (start us, length us, event | category | flops | bytes accessed | tf_op | source)
XLA Modules:
  0.0 370.6 jit_solution(6219848816667013529)
XLA Ops:
  7.2 4.9 %copy.52 = bf16[8,128,2048]{2,1,0:T(8,128)(2,1)} copy(bf16[8,128,2048]{2,1,0:T(8,128)(2,1)} %param.26) | data formatting | bytes 8388608
  12.1 9.4 %fusion.37 = f32[2048,2048]{1,0:T(8,128)} fusion(bf16[256,2048]{1,0:T(8,128)(2,1)S(1)} %copy-done, bf16[256,2048]{1,0:T(8,128)(2,1)} %param.16), kind=kOutput, calls=%fused_computation.137 | convolution fusion | flops 2147483648 | bytes 18874368 | tf_op jit(solution)/shard_map/dot_general | solution.py:46
  21.6 181.4 %reduce-scatter.2.cloned.1.call-done = f32[128,2048]{1,0:T(8,128)} async-done(((f32[2048,2048]{1,0:T(8,128)}), f32[128,2048]{1,0:T(8,128)}) %reduce-scatter.2.cloned.1.call-update) | async-done | bytes 1048592 | tf_op jit(solution)/shard_map/reduce_scatter | solution.py:96
  203.0 4.9 %fusion.35 = (bf16[128,2048]{1,0:T(8,128)(2,1)S(1)}, f32[128,2048]{1,0:T(8,128)}, f32[128,2048]{1,0:T(8,128)}, f32[128,2048]{1,0:T(8,128)}, f32[128,2048]{1,0:T(8,128)}) fusion(f32[128,2048]{1,0:T(8,128)S(1)} %copy-done.7, f32[128,2048]{1,0:T(8,128)} %param.17, f32[128,2048]{1,0:T(8,128)} %reduce-scatter.2.cloned.1.call-done, f32[128,2048]{1,0:T(8,128)} %param.18, ...), kind=kLoop, calls=%fused_computation.135 | loop fusion | flops 5242880 | bytes 9961472 | tf_op jit(solution)/shard_map/convert_element_type | solution.py:104
  207.9 11.3 %collective-permute-done = bf16[128,2048]{1,0:T(8,128)(2,1)S(1)} collective-permute-done((bf16[128,2048]{1,0:T(8,128)(2,1)S(1)}, bf16[128,2048]{1,0:T(8,128)(2,1)S(1)}, u32[]{:S(2)}, u32[]{:S(2)}) %collective-permute-start) | collective-permute-done | bytes 524320 | tf_op jit(solution)/shard_map/ppermute | solution.py:18
  219.2 4.4 %collective-permute-start.8 = (bf16[128,2048]{1,0:T(8,128)(2,1)S(1)}, bf16[128,2048]{1,0:T(8,128)(2,1)S(1)}, u32[]{:S(2)}, u32[]{:S(2)}) collective-permute-start(bf16[128,2048]{1,0:T(8,128)(2,1)S(1)} %get-tuple-element.14), channel_id=1, source_target_pairs={{0,15},{1,0},{2,1},{3,2},{4,3},{5,4},{6,5},{7,6},{8,7},{9,8},{10,9... | collective-permute-start | bytes 1572872 | tf_op jit(solution)/shard_map/ppermute | solution.py:20
  223.7 7.0 %collective-permute-done.1 = bf16[128,2048]{1,0:T(8,128)(2,1)S(1)} collective-permute-done((bf16[128,2048]{1,0:T(8,128)(2,1)S(1)}, bf16[128,2048]{1,0:T(8,128)(2,1)S(1)}, u32[]{:S(2)}, u32[]{:S(2)}) %collective-permute-start.1) | collective-permute-done | bytes 524320 | tf_op jit(solution)/shard_map/ppermute | solution.py:18
  230.6 4.4 %collective-permute-start.9 = (bf16[128,2048]{1,0:T(8,128)(2,1)S(1)}, bf16[128,2048]{1,0:T(8,128)(2,1)S(1)}, u32[]{:S(2)}, u32[]{:S(2)}) collective-permute-start(bf16[128,2048]{1,0:T(8,128)(2,1)S(1)} %collective-permute-done.8), channel_id=1, source_target_pairs={{0,15},{1,0},{2,1},{3,2},{4,3},{5,4},{6,5},{7,6},{8,7},{9,8},{10,9... | collective-permute-start | bytes 1572872 | tf_op jit(solution)/shard_map/ppermute | solution.py:20
  235.1 7.1 %collective-permute-done.2 = bf16[128,2048]{1,0:T(8,128)(2,1)} collective-permute-done((bf16[128,2048]{1,0:T(8,128)(2,1)S(1)}, bf16[128,2048]{1,0:T(8,128)(2,1)}, u32[]{:S(2)}, u32[]{:S(2)}) %collective-permute-start.2) | collective-permute-done | bytes 524320 | tf_op jit(solution)/shard_map/ppermute | solution.py:18
  242.2 4.4 %collective-permute-start.10 = (bf16[128,2048]{1,0:T(8,128)(2,1)S(1)}, bf16[128,2048]{1,0:T(8,128)(2,1)}, u32[]{:S(2)}, u32[]{:S(2)}) collective-permute-start(bf16[128,2048]{1,0:T(8,128)(2,1)S(1)} %collective-permute-done.9), channel_id=1, source_target_pairs={{0,15},{1,0},{2,1},{3,2},{4,3},{5,4},{6,5},{7,6},{8,7},{9,8},{10,9... | collective-permute-start | bytes 1572872 | tf_op jit(solution)/shard_map/ppermute | solution.py:20
  246.6 7.3 %collective-permute-done.3 = bf16[128,2048]{1,0:T(8,128)(2,1)} collective-permute-done((bf16[128,2048]{1,0:T(8,128)(2,1)}, bf16[128,2048]{1,0:T(8,128)(2,1)}, u32[]{:S(2)}, u32[]{:S(2)}) %collective-permute-start.3) | collective-permute-done | bytes 524320 | tf_op jit(solution)/shard_map/ppermute | solution.py:18
  253.9 1.7 collective-permute-start.4
  255.6 0.3 reduce_window_sum.34
  255.9 0.3 reduce_window_sum.36
  256.2 2.8 collective-permute-start.11
  258.9 6.6 %collective-permute-done.4 = bf16[128,2048]{1,0:T(8,128)(2,1)} collective-permute-done((bf16[128,2048]{1,0:T(8,128)(2,1)}, bf16[128,2048]{1,0:T(8,128)(2,1)}, u32[]{:S(2)}, u32[]{:S(2)}) %collective-permute-start.4) | collective-permute-done | bytes 524320 | tf_op jit(solution)/shard_map/ppermute | solution.py:18
  265.6 4.5 %collective-permute-start.5 = (bf16[128,2048]{1,0:T(8,128)(2,1)}, bf16[128,2048]{1,0:T(8,128)(2,1)}, u32[]{:S(2)}, u32[]{:S(2)}) collective-permute-start(bf16[128,2048]{1,0:T(8,128)(2,1)} %collective-permute-done.4), channel_id=1, source_target_pairs={{0,1},{1,2},{2,3},{3,4},{4,5},{5,6},{6,7},{7,8},{8,9},{9,10},{10,1... | collective-permute-start | bytes 1572872 | tf_op jit(solution)/shard_map/ppermute | solution.py:18
  270.2 8.0 %scatter_custom_fusion = s32[129]{0:T(256)S(1)} fusion(s32[2048]{0:T(1024)S(1)} %get-tuple-element.27, s32[2048]{0:T(1024)S(1)} %get-tuple-element.28, s32[]{:T(128)} %constant.124.clone.1), kind=kCustom, calls=%fused_computation.131 | custom fusion | bytes 520 | tf_op jit(solution)/shard_map/scatter | solution.py:36
  278.3 0.9 gather_fusion
  279.3 2.5 collective-permute-start.6
  281.8 0.9 select_bitcast_fusion.1
  282.7 9.0 %all-to-all-start = ((bf16[16,8,2048]{2,1,0:T(8,128)(2,1)}), bf16[16,8,2048]{2,1,0:T(8,128)(2,1)S(1)}, u32[]{:S(2)}, u32[]{:S(2)}) async-start(bf16[16,8,2048]{2,1,0:T(8,128)(2,1)} %select_bitcast_fusion.1), calls=%async_computation.1 | async-start | bytes 1048576 | tf_op jit(solution)/shard_map/all_to_all | solution.py:91
  291.8 0.1 and_select_fusion
  291.8 0.1 fusion.12
  291.9 0.2 reduce_window_sum.35
  292.1 0.2 select_reduce_fusion.1
  292.3 4.4 %collective-permute-start.13 = (bf16[128,2048]{1,0:T(8,128)(2,1)}, bf16[128,2048]{1,0:T(8,128)(2,1)}, u32[]{:S(2)}, u32[]{:S(2)}) collective-permute-start(bf16[128,2048]{1,0:T(8,128)(2,1)} %collective-permute-done.12), channel_id=1, source_target_pairs={{0,15},{1,0},{2,1},{3,2},{4,3},{5,4},{6,5},{7,6},{8,7},{9,8},{10,9... | collective-permute-start | bytes 1572872 | tf_op jit(solution)/shard_map/ppermute | solution.py:20
  296.7 1.9 collective-permute-start.7
  298.7 8.0 %scatter_custom_fusion.1 = s32[129]{0:T(256)S(1)} fusion(s32[2048]{0:T(1024)S(1)} %get-tuple-element.20, s32[2048]{0:T(1024)S(1)} %get-tuple-element.19, s32[]{:T(128)} %constant.124.clone.1), kind=kCustom, calls=%fused_computation.129 | custom fusion | bytes 520 | tf_op jit(solution)/shard_map/scatter | solution.py:36
  306.8 0.9 gather_fusion.1
  307.7 7.9 %collective-permute-start.14 = (bf16[128,2048]{1,0:T(8,128)(2,1)}, bf16[128,2048]{1,0:T(8,128)(2,1)S(1)}, u32[]{:S(2)}, u32[]{:S(2)}) collective-permute-start(bf16[128,2048]{1,0:T(8,128)(2,1)} %collective-permute-done.13), channel_id=1, source_target_pairs={{0,15},{1,0},{2,1},{3,2},{4,3},{5,4},{6,5},{7,6},{8,7},{9,8},{10,9... | collective-permute-start | bytes 1572872 | tf_op jit(solution)/shard_map/ppermute | solution.py:20
  315.7 1.1 constant_dynamic-update-slice_fusion.31
  316.7 1.1 constant_dynamic-update-slice_fusion.30
  317.8 1.1 constant_dynamic-update-slice_fusion.29
  318.9 1.1 constant_dynamic-update-slice_fusion.28
  320.0 1.1 constant_dynamic-update-slice_fusion.27
  321.1 1.1 constant_dynamic-update-slice_fusion.26
  322.2 1.1 constant_dynamic-update-slice_fusion.25
  323.4 1.1 constant_dynamic-update-slice_fusion.21
  324.5 1.1 constant_dynamic-update-slice_fusion.20
  325.6 1.1 constant_dynamic-update-slice_fusion.19
  326.7 1.1 constant_dynamic-update-slice_fusion.18
  327.8 1.1 constant_dynamic-update-slice_fusion.17
  329.0 1.1 constant_dynamic-update-slice_fusion.15
  330.1 1.1 constant_dynamic-update-slice_fusion.14
  331.2 1.1 constant_dynamic-update-slice_fusion.13
  332.2 1.1 constant_dynamic-update-slice_fusion.12
  333.3 1.1 constant_dynamic-update-slice_fusion.11
  334.4 1.1 constant_dynamic-update-slice_fusion.10
  335.8 1.2 constant_dynamic-update-slice_fusion.4
  337.0 1.1 constant_dynamic-update-slice_fusion.3
  338.1 1.1 constant_dynamic-update-slice_fusion.2
  339.2 1.1 constant_dynamic-update-slice_fusion.1
  340.3 1.3 fusion.36
  341.6 0.1 multiply_reduce_fusion
  341.8 0.2 maximum_convert_fusion
  342.0 0.9 gather_fusion.2
  343.0 0.9 select_bitcast_fusion
  343.9 3.6 all-to-all-start.1
  347.5 0.2 reduce_window_sum.37
  348.4 0.2 select_reduce_fusion
  348.6 13.3 %all-to-all-done.1 = bf16[16,8,2048]{2,1,0:T(8,128)(2,1)S(1)} async-done(((bf16[16,8,2048]{2,1,0:T(8,128)(2,1)}), bf16[16,8,2048]{2,1,0:T(8,128)(2,1)S(1)}, u32[]{:S(2)}, u32[]{:S(2)}) %all-to-all-start.1) | async-done | bytes 524320 | tf_op jit(solution)/shard_map/all_to_all | solution.py:109
  361.9 0.9 gather_fusion.3
  362.8 1.0 bitcast_dynamic-update-slice_fusion
  (67 shorter events, 0.9 us)
Async XLA Ops:
  7.2 4.9 %copy-start = (bf16[256,2048]{1,0:T(8,128)(2,1)S(1)}, bf16[256,2048]{1,0:T(8,128)(2,1)}, u32[]{:S(2)}) copy-start(bf16[256,2048]{1,0:T(8,128)(2,1)} %param.15) | copy-start | bytes 3145732
  7.2 195.8 %reduce-scatter.2.cloned.1.call-start = ((), (), s32[]{:S(2)}) async-start(), calls=%async_computation.3 | async-start | bytes 17825792 | tf_op jit(solution)/shard_map/reduce_scatter | solution.py:96
  12.1 190.9 %copy-start.7 = (f32[128,2048]{1,0:T(8,128)S(1)}, f32[128,2048]{1,0:T(8,128)}, u32[]{:S(2)}) copy-start(f32[128,2048]{1,0:T(8,128)} %param.20) | copy-start | bytes 3145732
  21.5 234.0 %copy-start.9 = (s32[2048]{0:T(1024)S(1)}, s32[2048]{0:T(1024)}, u32[]{:S(2)}) copy-start(s32[2048]{0:T(1024)} %param.22) | copy-start | bytes 24580
  21.5 234.3 %copy-start.8 = (s32[2048]{0:T(1024)S(1)}, s32[2048]{0:T(1024)}, u32[]{:S(2)}) copy-start(s32[2048]{0:T(1024)} %param.23) | copy-start | bytes 24580
  21.5 256.7 %copy-start.2 = (bf16[128,2048]{1,0:T(8,128)(2,1)S(1)}, bf16[128,2048]{1,0:T(8,128)(2,1)}, u32[]{:S(2)}) copy-start(bf16[128,2048]{1,0:T(8,128)(2,1)} %param.21) | copy-start | bytes 1572868
  207.9 11.3 %collective-permute-start = (bf16[128,2048]{1,0:T(8,128)(2,1)S(1)}, bf16[128,2048]{1,0:T(8,128)(2,1)S(1)}, u32[]{:S(2)}, u32[]{:S(2)}) collective-permute-start(bf16[128,2048]{1,0:T(8,128)(2,1)S(1)} %get-tuple-element.14), channel_id=1, source_target_pairs={{0,1},{1,2},{2,3},{3,4},{4,5},{5,6},{6,7},{7,8},{8,9},{9,10},{10,1... | collective-permute-start | bytes 1572872 | tf_op jit(solution)/shard_map/ppermute | solution.py:18
  219.2 11.4 %collective-permute-start.1 = (bf16[128,2048]{1,0:T(8,128)(2,1)S(1)}, bf16[128,2048]{1,0:T(8,128)(2,1)S(1)}, u32[]{:S(2)}, u32[]{:S(2)}) collective-permute-start(bf16[128,2048]{1,0:T(8,128)(2,1)S(1)} %collective-permute-done), channel_id=1, source_target_pairs={{0,1},{1,2},{2,3},{3,4},{4,5},{5,6},{6,7},{7,8},{8,9},{9,10},{10,1... | collective-permute-start | bytes 1572872 | tf_op jit(solution)/shard_map/ppermute | solution.py:18
  219.2 11.4 %collective-permute-start.8 = (bf16[128,2048]{1,0:T(8,128)(2,1)S(1)}, bf16[128,2048]{1,0:T(8,128)(2,1)S(1)}, u32[]{:S(2)}, u32[]{:S(2)}) collective-permute-start(bf16[128,2048]{1,0:T(8,128)(2,1)S(1)} %get-tuple-element.14), channel_id=1, source_target_pairs={{0,15},{1,0},{2,1},{3,2},{4,3},{5,4},{6,5},{7,6},{8,7},{9,8},{10,9... | collective-permute-start | bytes 1572872 | tf_op jit(solution)/shard_map/ppermute | solution.py:20
  230.6 47.6 %copy-start.3 = (bf16[128,2048]{1,0:T(8,128)(2,1)}, bf16[128,2048]{1,0:T(8,128)(2,1)S(1)}, u32[]{:S(2)}) copy-start(bf16[128,2048]{1,0:T(8,128)(2,1)S(1)} %collective-permute-done.1) | copy-start | bytes 1572868
  230.6 11.5 %collective-permute-start.2 = (bf16[128,2048]{1,0:T(8,128)(2,1)S(1)}, bf16[128,2048]{1,0:T(8,128)(2,1)}, u32[]{:S(2)}, u32[]{:S(2)}) collective-permute-start(bf16[128,2048]{1,0:T(8,128)(2,1)S(1)} %collective-permute-done.1), channel_id=1, source_target_pairs={{0,1},{1,2},{2,3},{3,4},{4,5},{5,6},{6,7},{7,8},{8,9},{9,10},{10,1... | collective-permute-start | bytes 1572872 | tf_op jit(solution)/shard_map/ppermute | solution.py:18
  230.6 11.5 %collective-permute-start.9 = (bf16[128,2048]{1,0:T(8,128)(2,1)S(1)}, bf16[128,2048]{1,0:T(8,128)(2,1)S(1)}, u32[]{:S(2)}, u32[]{:S(2)}) collective-permute-start(bf16[128,2048]{1,0:T(8,128)(2,1)S(1)} %collective-permute-done.8), channel_id=1, source_target_pairs={{0,15},{1,0},{2,1},{3,2},{4,3},{5,4},{6,5},{7,6},{8,7},{9,8},{10,9... | collective-permute-start | bytes 1572872 | tf_op jit(solution)/shard_map/ppermute | solution.py:20
  242.1 11.7 %collective-permute-start.3 = (bf16[128,2048]{1,0:T(8,128)(2,1)}, bf16[128,2048]{1,0:T(8,128)(2,1)}, u32[]{:S(2)}, u32[]{:S(2)}) collective-permute-start(bf16[128,2048]{1,0:T(8,128)(2,1)} %collective-permute-done.2), channel_id=1, source_target_pairs={{0,1},{1,2},{2,3},{3,4},{4,5},{5,6},{6,7},{7,8},{8,9},{9,10},{10,1... | collective-permute-start | bytes 1572872 | tf_op jit(solution)/shard_map/ppermute | solution.py:18
  242.1 64.6 %copy-start.5 = (bf16[128,2048]{1,0:T(8,128)(2,1)}, bf16[128,2048]{1,0:T(8,128)(2,1)S(1)}, u32[]{:S(2)}) copy-start(bf16[128,2048]{1,0:T(8,128)(2,1)S(1)} %collective-permute-done.9) | copy-start | bytes 1572868
  242.2 14.0 %collective-permute-start.10 = (bf16[128,2048]{1,0:T(8,128)(2,1)S(1)}, bf16[128,2048]{1,0:T(8,128)(2,1)}, u32[]{:S(2)}, u32[]{:S(2)}) collective-permute-start(bf16[128,2048]{1,0:T(8,128)(2,1)S(1)} %collective-permute-done.9), channel_id=1, source_target_pairs={{0,15},{1,0},{2,1},{3,2},{4,3},{5,4},{6,5},{7,6},{8,7},{9,8},{10,9... | collective-permute-start | bytes 1572872 | tf_op jit(solution)/shard_map/ppermute | solution.py:20
  253.9 11.7 %collective-permute-start.4 = (bf16[128,2048]{1,0:T(8,128)(2,1)}, bf16[128,2048]{1,0:T(8,128)(2,1)}, u32[]{:S(2)}, u32[]{:S(2)}) collective-permute-start(bf16[128,2048]{1,0:T(8,128)(2,1)} %collective-permute-done.3), channel_id=1, source_target_pairs={{0,1},{1,2},{2,3},{3,4},{4,5},{5,6},{6,7},{7,8},{8,9},{9,10},{10,1... | collective-permute-start | bytes 1572872 | tf_op jit(solution)/shard_map/ppermute | solution.py:18
  256.2 23.0 %collective-permute-start.11 = (bf16[128,2048]{1,0:T(8,128)(2,1)}, bf16[128,2048]{1,0:T(8,128)(2,1)}, u32[]{:S(2)}, u32[]{:S(2)}) collective-permute-start(bf16[128,2048]{1,0:T(8,128)(2,1)} %collective-permute-done.10), channel_id=1, source_target_pairs={{0,15},{1,0},{2,1},{3,2},{4,3},{5,4},{6,5},{7,6},{8,7},{9,8},{10,9... | collective-permute-start | bytes 1572872 | tf_op jit(solution)/shard_map/ppermute | solution.py:20
  265.6 13.7 %collective-permute-start.5 = (bf16[128,2048]{1,0:T(8,128)(2,1)}, bf16[128,2048]{1,0:T(8,128)(2,1)}, u32[]{:S(2)}, u32[]{:S(2)}) collective-permute-start(bf16[128,2048]{1,0:T(8,128)(2,1)} %collective-permute-done.4), channel_id=1, source_target_pairs={{0,1},{1,2},{2,3},{3,4},{4,5},{5,6},{6,7},{7,8},{8,9},{9,10},{10,1... | collective-permute-start | bytes 1572872 | tf_op jit(solution)/shard_map/ppermute | solution.py:18
  279.2 13.1 %collective-permute-start.12 = (bf16[128,2048]{1,0:T(8,128)(2,1)}, bf16[128,2048]{1,0:T(8,128)(2,1)}, u32[]{:S(2)}, u32[]{:S(2)}) collective-permute-start(bf16[128,2048]{1,0:T(8,128)(2,1)} %collective-permute-done.11), channel_id=1, source_target_pairs={{0,15},{1,0},{2,1},{3,2},{4,3},{5,4},{6,5},{7,6},{8,7},{9,8},{10,9... | collective-permute-start | bytes 1572872 | tf_op jit(solution)/shard_map/ppermute | solution.py:20
  279.3 17.4 %collective-permute-start.6 = (bf16[128,2048]{1,0:T(8,128)(2,1)}, bf16[128,2048]{1,0:T(8,128)(2,1)}, u32[]{:S(2)}, u32[]{:S(2)}) collective-permute-start(bf16[128,2048]{1,0:T(8,128)(2,1)} %collective-permute-done.5), channel_id=1, source_target_pairs={{0,1},{1,2},{2,3},{3,4},{4,5},{5,6},{6,7},{7,8},{8,9},{9,10},{10,1... | collective-permute-start | bytes 1572872 | tf_op jit(solution)/shard_map/ppermute | solution.py:18
  282.7 52.8 %copy-start.4 = (bf16[128,2048]{1,0:T(8,128)(2,1)S(1)}, bf16[128,2048]{1,0:T(8,128)(2,1)}, u32[]{:S(2)}) copy-start(bf16[128,2048]{1,0:T(8,128)(2,1)} %copy-done.3) | copy-start | bytes 1572868
  282.7 24.0 %all-to-all-start = ((bf16[16,8,2048]{2,1,0:T(8,128)(2,1)}), bf16[16,8,2048]{2,1,0:T(8,128)(2,1)S(1)}, u32[]{:S(2)}, u32[]{:S(2)}) async-start(bf16[16,8,2048]{2,1,0:T(8,128)(2,1)} %select_bitcast_fusion.1), calls=%async_computation.1 | async-start | bytes 1048576 | tf_op jit(solution)/shard_map/all_to_all | solution.py:91
  292.3 15.4 %collective-permute-start.13 = (bf16[128,2048]{1,0:T(8,128)(2,1)}, bf16[128,2048]{1,0:T(8,128)(2,1)}, u32[]{:S(2)}, u32[]{:S(2)}) collective-permute-start(bf16[128,2048]{1,0:T(8,128)(2,1)} %collective-permute-done.12), channel_id=1, source_target_pairs={{0,15},{1,0},{2,1},{3,2},{4,3},{5,4},{6,5},{7,6},{8,7},{9,8},{10,9... | collective-permute-start | bytes 1572872 | tf_op jit(solution)/shard_map/ppermute | solution.py:20
  296.7 18.9 %collective-permute-start.7 = (bf16[128,2048]{1,0:T(8,128)(2,1)}, bf16[128,2048]{1,0:T(8,128)(2,1)}, u32[]{:S(2)}, u32[]{:S(2)}) collective-permute-start(bf16[128,2048]{1,0:T(8,128)(2,1)} %collective-permute-done.6), channel_id=1, source_target_pairs={{0,1},{1,2},{2,3},{3,4},{4,5},{5,6},{6,7},{7,8},{8,9},{9,10},{10,1... | collective-permute-start | bytes 1572872 | tf_op jit(solution)/shard_map/ppermute | solution.py:18
  307.7 28.0 %copy-start.6 = (bf16[128,2048]{1,0:T(8,128)(2,1)S(1)}, bf16[128,2048]{1,0:T(8,128)(2,1)}, u32[]{:S(2)}) copy-start(bf16[128,2048]{1,0:T(8,128)(2,1)} %copy-done.5) | copy-start | bytes 1572868
  307.7 21.2 %collective-permute-start.14 = (bf16[128,2048]{1,0:T(8,128)(2,1)}, bf16[128,2048]{1,0:T(8,128)(2,1)S(1)}, u32[]{:S(2)}, u32[]{:S(2)}) collective-permute-start(bf16[128,2048]{1,0:T(8,128)(2,1)} %collective-permute-done.13), channel_id=1, source_target_pairs={{0,15},{1,0},{2,1},{3,2},{4,3},{5,4},{6,5},{7,6},{8,7},{9,8},{10,9... | collective-permute-start | bytes 1572872 | tf_op jit(solution)/shard_map/ppermute | solution.py:20
  324.5 17.3 %copy-start.10 = (f32[2048]{0:T(1024)S(1)}, f32[2048]{0:T(1024)}, u32[]{:S(2)}) copy-start(f32[2048]{0:T(1024)} %param.25) | copy-start | bytes 24580
  324.5 17.3 %copy-start.11 = (f32[2048]{0:T(1024)S(1)}, f32[2048]{0:T(1024)}, u32[]{:S(2)}) copy-start(f32[2048]{0:T(1024)} %param.24) | copy-start | bytes 24580
  335.6 28.2 %copy-start.1 = (bf16[256,2048]{1,0:T(8,128)(2,1)S(1)}, bf16[256,2048]{1,0:T(8,128)(2,1)}, u32[]{:S(2)}) copy-start(bf16[256,2048]{1,0:T(8,128)(2,1)} %param.15) | copy-start | bytes 3145732
  343.9 18.0 %all-to-all-start.1 = ((bf16[16,8,2048]{2,1,0:T(8,128)(2,1)}), bf16[16,8,2048]{2,1,0:T(8,128)(2,1)S(1)}, u32[]{:S(2)}, u32[]{:S(2)}) async-start(bf16[16,8,2048]{2,1,0:T(8,128)(2,1)} %select_bitcast_fusion), calls=%async_computation.2 | async-start | bytes 1048576 | tf_op jit(solution)/shard_map/all_to_all | solution.py:109
Sparse Core Ops, SparseCore 0:
  21.7 181.2 reduce-scatter.1
